TPU v7x, 32 devices: a whole 2x2x4 slice. The times are simulated.
32 devices in a mesh: seq: 8 (over z, x), head: 4 (over y, core).
Axes of the slice: x: 2, y: 2, z: 4, core: 2. Of those that a mesh axis runs over, the one named last changes fastest.
Arguments:
- queries: float32 [8192, 2048], P('seq', 'head')
- keys: float32 [8192, 2048], P('seq', 'head')
- values: float32 [8192, 2048], P('seq', 'head'), may hold values from -6 to 6
- positions: int32 [8192], P('seq'), may hold values from 0 to 8191, as said below
- cluster: int32 [8192], P('seq'), may hold values from 0 to 7, as said below
- slot: int32 [8192], P('seq'), may hold values from 0 to 1023, as said below
- out_weight: float32 [2048, 4096], P('head'), may hold values from -0.5 to 0.5
Outputs:
- projected: float32 [8192, 4096], P('seq', 'head')
Inputs may be any that keep to these rules, and one draw needn't show every extreme that they name: Every cluster holds exactly 1024 tokens. Of the tokens of one index of seq, at most 192 have cluster ids in one range k * 1 to (k + 1) - 1. Within each cluster every slot is taken once, in increasing order of position. `positions`: each position is taken by exactly one token.
All inputs are finite; a program needn't handle non-finite values.
Results may differ from a plain program's by a relative error of at most 0.0003.
Values sent between devices are 32-bit elements; how exact they have to be, the bound alone decides.
No kernel may reach another device: no remote copies, remote signals or barrier semaphores. Data moves between devices by JAX's collectives and lax.ppermute only.
A program may use at most 128 MiB of HBM per device.

v0:
```python
import math
import jax
import jax.numpy as jnp
from jax import lax
from jax.sharding import PartitionSpec as P

DH = 128
CS = 1024
CL_DEV = 1
ROPE_BASE = 500000.0
ORIG_CONTEXT = 8192.0
STRETCH = 4.0
BETA_FAST = 32.0
BETA_SLOW = 1.0


def yarn_tables(token_pos, width):
    half_width = width // 2
    expo = jnp.arange(half_width, dtype=jnp.float32) * 2.0 / width
    theta = jnp.exp(-expo * math.log(ROPE_BASE))
    ratio = ORIG_CONTEXT * theta / (2.0 * math.pi)
    ramp = jnp.clip((ratio - BETA_SLOW) / (BETA_FAST - BETA_SLOW), 0.0, 1.0)
    freq = theta * (ramp + (1.0 - ramp) / STRETCH)
    angle = token_pos.astype(jnp.float32)[:, None] * freq[None, :]
    mscale = 0.1 * math.log(STRETCH) + 1.0
    cos_table = jnp.concatenate([jnp.cos(angle), jnp.cos(angle)], -1) * mscale
    sin_table = jnp.concatenate([jnp.sin(angle), jnp.sin(angle)], -1) * mscale
    return (cos_table[:, None, :], sin_table[:, None, :])


def rotate(field, cos_table, sin_table):
    half_width = field.shape[-1] // 2
    turned = jnp.concatenate([-field[..., half_width:], field[..., :half_width]], -1)
    return field * cos_table + turned * sin_table


def cluster_attention(triple):
    query_c, key_c, value_c = triple
    length = query_c.shape[0]
    scores = jnp.einsum(
        "qhd,khd->hqk", query_c, key_c, precision=lax.Precision.HIGHEST
    ) / math.sqrt(query_c.shape[-1])
    causal = jnp.arange(length)[:, None] >= jnp.arange(length)[None, :]
    scores = jnp.where(causal[None], scores, -jnp.inf)
    peak = jnp.max(scores, -1, keepdims=True)
    weights = jnp.exp(scores - peak)
    total = jnp.sum(weights, -1, keepdims=True)
    summed = jnp.einsum("hqk,khd->qhd", weights, value_c, precision=lax.Precision.HIGHEST)
    return summed / jnp.transpose(total, (1, 0, 2))


def attend_local(query_all, key_all, value_all):
    row_count, head_count, width = query_all.shape
    grouped = (
        query_all.reshape(row_count // CS, CS, head_count, width),
        key_all.reshape(row_count // CS, CS, head_count, width),
        value_all.reshape(row_count // CS, CS, head_count, width),
    )
    return lax.map(cluster_attention, grouped).reshape(row_count, head_count, width)


def per_device(queries, keys, values, positions, cluster, slot, out_weight):
    seq_count = lax.axis_size("seq")
    head_count = lax.axis_size("head")
    head_index = lax.axis_index("head")
    col_width = out_weight.shape[1] // head_count
    weight_blocks = out_weight.reshape(out_weight.shape[0], head_count, col_width)
    weight_parts = [None] * head_count
    for shift in range(head_count):
        if shift == 0:
            piece = weight_blocks[:, head_index]
        else:
            dest = (head_index + shift) % head_count
            piece = lax.ppermute(
                jnp.take(weight_blocks, dest, axis=1),
                "head",
                [(src, (src + shift) % head_count) for src in range(head_count)],
            )
        weight_parts[shift] = piece
    stacked_w = jnp.stack(weight_parts, 0)
    order = (head_index - jnp.arange(head_count)) % head_count
    weight_cols = stacked_w[order].reshape(head_count * out_weight.shape[0], col_width)
    row_count = queries.shape[0]
    capacity = 3 * row_count // (2 * seq_count)
    buffer_rows = seq_count * capacity
    heads_here = queries.shape[1] // DH
    owner_ids = cluster // CL_DEV
    target_row = cluster % CL_DEV * CS + slot
    one_hot = (owner_ids[:, None] == jnp.arange(seq_count)[None, :]).astype(jnp.int32)
    token_rank = jnp.sum(jnp.cumsum(one_hot, 0) * one_hot, 1) - 1
    send_row = owner_ids * capacity + token_rank
    source_token = (
        jnp.full((buffer_rows,), row_count, jnp.int32)
        .at[send_row]
        .set(jnp.arange(row_count, dtype=jnp.int32))
    )
    cos_table, sin_table = yarn_tables(positions, DH)
    shaped = (row_count, heads_here, DH)
    rot_q = rotate(queries.reshape(shaped), cos_table, sin_table)
    rot_k = rotate(keys.reshape(shaped), cos_table, sin_table)
    stacked = jnp.concatenate([rot_q, rot_k, values.reshape(shaped)], 1)
    stacked = jnp.concatenate([stacked, jnp.zeros((1, 3 * heads_here, DH), jnp.float32)], 0)
    send_all = stacked[source_token]
    send_q = send_all[:, :heads_here]
    send_k = send_all[:, heads_here : 2 * heads_here]
    send_v = send_all[:, 2 * heads_here :]
    slot_rows = jnp.full((buffer_rows,), row_count, jnp.int32).at[send_row].set(target_row)
    arrived = lax.all_to_all(slot_rows, "seq", split_axis=0, concat_axis=0, tiled=True)
    picked = jnp.minimum(arrived, row_count - 1)
    where_from = (
        jnp.zeros((row_count,), jnp.int32)
        .at[arrived]
        .set(jnp.arange(buffer_rows, dtype=jnp.int32), mode="drop")
    )

    def place(pieces):
        return pieces[where_from]

    received = (
        lax.all_to_all(send_q, "seq", split_axis=0, concat_axis=0, tiled=True),
        lax.all_to_all(send_k, "seq", split_axis=0, concat_axis=0, tiled=True),
        lax.all_to_all(send_v, "seq", split_axis=0, concat_axis=0, tiled=True),
    )
    result = attend_local(place(received[0]), place(received[1]), place(received[2]))
    result, weight_cols = lax.optimization_barrier((result, weight_cols))
    returned = lax.all_to_all(result[picked], "seq", split_axis=0, concat_axis=0, tiled=True)
    mixed = returned[send_row].reshape(row_count, heads_here * DH)
    gathered = lax.all_gather(mixed, "head", axis=1, tiled=True)
    projected = jnp.dot(
        gathered, weight_cols, precision=lax.Precision.HIGHEST, preferred_element_type=jnp.float32
    )
    return projected


def solution(mesh):
    in_specs = (
        P("seq", "head"),
        P("seq", "head"),
        P("seq", "head"),
        P("seq"),
        P("seq"),
        P("seq"),
        P("head", None),
    )
    out_specs = P("seq", "head")
    return jax.shard_map(
        per_device, mesh=mesh, in_specs=in_specs, out_specs=out_specs, check_vma=False
    )
```

profile of v0, /device:TPU:0, one launch (start us, length us, event | category | flops | bytes accessed | tf_op | source)
XLA Modules:
  0.0 617.9 jit_solution(9982841143723869538)
XLA Ops:
  6.5 0.7 fusion.19
  7.2 2.3 reduce-window.6
  10.0 0.7 fusion.18
  10.7 0.7 broadcast_clamp_fusion
  11.4 4.5 scatter_custom_fusion.1
  15.9 0.7 all_to_all.27
  16.6 7.3 %all-to-all-start.1 = ((s32[8,192,1]{1,2,0:T(1,128)}), s32[8,192,1]{1,2,0:T(1,128)S(1)}, u32[]{:S(2)}, u32[]{:S(2)}) async-start(s32[8,192,1]{1,2,0:T(1,128)} %all_to_all.27), calls=%async_computation.1 | async-start | bytes 16384 | tf_op jit(solution)/shard_map/all_to_all | solution.py:108
  23.8 2.9 reshape.229
  26.7 1.9 reshape.228
  28.7 3.0 reshape.227
  31.6 4.8 scatter_custom_fusion
  36.5 4.6 slice_negate_fusion
  41.2 1.9 multiply_cosine_fusion
  43.4 3.0 fusion.7
  46.5 5.3 select_maximum_fusion
  51.8 12.0 %gather_fusion = f32[1536,12,128]{2,1,0:T(8,128)} fusion(f32[1025,12,128]{2,1,0:T(8,128)} %select_maximum_fusion, s32[2048]{0:T(1024)S(1)} %pad_clamp_fusion.1), kind=kCustom, calls=%fused_computation | custom fusion | bytes 18880512 | tf_op jit(solution)/shard_map/gather | solution.py:103
  63.8 10.0 %fusion.33 = (f32[1536,4,128]{2,1,0:T(4,128)}, f32[1536,4,128]{2,1,0:T(4,128)}, f32[1536,4,128]{2,1,0:T(4,128)S(1)}) fusion(f32[1536,12,128]{2,1,0:T(8,128)} %gather_fusion), kind=kLoop, calls=%fused_computation.85 | loop fusion | bytes 18874368 | tf_op jit(solution)/shard_map/slice | solution.py:106
  73.8 76.2 %all_to_all.33 = f32[1536,4,128]{2,1,0:T(4,128)} all-to-all(f32[1536,4,128]{2,1,0:T(4,128)S(1)} %get-tuple-element.42), channel_id=1, replica_groups=mesh['seq'=8,'head'=4] {'seq'}, dimensions={0} | all-to-all | bytes 6291456 | tf_op jit(solution)/shard_map/all_to_all | solution.py:121
  149.9 3.8 all-to-all-start.2
  153.8 10.8 %reshape.231 = f32[512,4,1024]{2,1,0:T(4,128)} reshape(f32[512,4096]{1,0:T(8,128)} %param.15) | data formatting | bytes 16777216 | tf_op jit(solution)/shard_map/reshape | solution.py:67
  164.6 59.2 %all-to-all-done.2 = f32[1536,4,128]{2,1,0:T(4,128)S(1)} async-done(((f32[1536,4,128]{2,1,0:T(4,128)}), f32[1536,4,128]{2,1,0:T(4,128)S(1)}, u32[]{:S(2)}, u32[]{:S(2)}) %all-to-all-start.2) | async-done | bytes 3145760 | tf_op jit(solution)/shard_map/all_to_all | solution.py:120
  223.8 1.7 copy-done.2
  225.5 4.5 all-to-all-start
  230.1 20.0 %constant_dynamic-slice_fusion.2 = (f32[512,1,1024]{2,1,0:T(1,128)}, f32[512,1,1024]{2,1,0:T(1,128)S(1)}, f32[512,1,1024]{2,1,0:T(1,128)S(1)}, f32[512,1,1024]{2,1,0:T(1,128)}) fusion(f32[512,4,1024]{2,1,0:T(4,128)} %reshape.231, s32[]{:T(128)S(6)} %select_n.98, s32[]{:T(128)S(6)} %select_n.115, s32[]{:T(128)S(6)} %select_n.119, pred[]{:T(512)S(6)} %and.53, ...), kind=kLoop, calls=%fused_computation.79 | loop fusion | flops 524288 | bytes 16777232 | tf_op jit(solution)/shard_map/dynamic_slice | solution.py:71
  250.1 1.8 copy.56
  251.9 3.5 fusion.9
  255.4 1.5 collective-permute-start.1
  256.9 1.8 fusion.10
  259.9 6.2 scatter_custom_fusion.2
  266.1 27.5 %collective-permute-done.2 = f32[512,1024]{1,0:T(8,128)} collective-permute-done((f32[512,1024]{1,0:T(8,128)}, f32[512,1024]{1,0:T(8,128)}, u32[]{:S(2)}, u32[]{:S(2)}) %collective-permute-start.2) | collective-permute-done | bytes 2097184 | tf_op jit(solution)/shard_map/ppermute | solution.py:74
  293.6 47.9 %collective-permute-done.1 = f32[512,1024]{1,0:T(8,128)} collective-permute-done((f32[512,1024]{1,0:T(8,128)}, f32[512,1024]{1,0:T(8,128)}, u32[]{:S(2)}, u32[]{:S(2)}) %collective-permute-start.1) | collective-permute-done | bytes 2097184 | tf_op jit(solution)/shard_map/ppermute | solution.py:74
  341.5 3.6 collective-permute-done
  345.1 5.8 pad_maximum_fusion
  350.9 7.7 %gather_fusion.4 = f32[4,512,1024]{2,1,0:T(8,128)} fusion(f32[4,512,1024]{2,1,0:T(8,128)} %pad_maximum_fusion, s32[1024]{0:T(1024)S(1)} %pad_clamp_fusion.2), kind=kCustom, calls=%fused_computation.4 | custom fusion | bytes 16777232 | tf_op jit(solution)/shard_map/gather | solution.py:82
  358.6 5.4 gather_fusion.3
  364.0 9.8 %gather_fusion.2 = f32[1024,4,128]{2,1,0:T(4,128)} fusion(f32[1536,4,128]{2,1,0:T(4,128)} %copy-done.2, s32[1024]{0:T(1024)S(1)} %fusion.22), kind=kCustom, calls=%fused_computation.2 | custom fusion | bytes 4198400 | tf_op jit(solution)/shard_map/gather | solution.py:117
  373.9 20.7 %fusion = (f32[4,1024]{1,0:T(4,128)S(1)}, f32[4,1024,1024]{1,2,0:T(8,128)S(1)}) fusion(pred[1024,1024]{0,1:T(8,128)(4,1)S(1)} %iota_compare_fusion.1, f32[1024,4,128]{2,1,0:T(4,128)S(1)} %gather_fusion.3, f32[1024,4,128]{2,1,0:T(4,128)} %gather_fusion.2), kind=kOutput, calls=%fused_computation.12 | convolution fusion | flops 6455029760 | bytes 22036480 | tf_op jit(solution)/shard_map/while/body/eval_jaxpr/qhd,khd->hqk/dot_general | solution.py:40
  394.5 5.7 copy-done
  400.2 3.6 fusion.1
  403.9 5.4 gather_fusion.1
  409.3 18.2 %bitcast_divide_fusion = f32[1024,4,128]{0,2,1:T(8,128)} fusion(f32[1024,4]{0,1:T(4,128)S(1)} %bitcast.51, f32[4,1024,1024]{1,2,0:T(8,128)} %copy-done, f32[4,1024]{1,0:T(4,128)S(1)} %get-tuple-element.55, pred[1024,1024]{0,1:T(8,128)(4,1)S(1)} %iota_compare_fusion.1, f32[1024,4,128]{2,1,0:T(4,128)S(1)} %gather_fusion.1), kind=kOutput, calls=%fused_computation.38 | convolution fusion | flops 6455558144 | bytes 22052864 | tf_op jit(solution)/shard_map/while/body/eval_jaxpr/hqk,khd->qhd/dot_general | solution.py:48
  427.5 2.0 copy.25
  429.6 5.5 gather_fusion.5
  435.0 75.1 %all_to_all.34 = f32[1536,4,128]{2,1,0:T(4,128)S(1)} all-to-all(f32[1536,4,128]{2,1,0:T(4,128)} %gather_fusion.5), channel_id=1, replica_groups=mesh['seq'=8,'head'=4] {'seq'}, dimensions={0} | all-to-all | bytes 6291456 | tf_op jit(solution)/shard_map/all_to_all | solution.py:126
  510.2 7.9 %gather_fusion.6 = f32[1024,4,128]{2,1,0:T(4,128)} fusion(f32[1536,4,128]{2,1,0:T(4,128)S(1)} %all_to_all.34, s32[1024]{0:T(1024)S(1)} %get-tuple-element.38), kind=kCustom, calls=%fused_computation.6 | custom fusion | bytes 4198400 | tf_op jit(solution)/shard_map/gather | solution.py:127
  518.1 3.2 copy.55
  521.3 57.5 %all-gather.2.cloned.1.call-done = f32[1024,2048]{1,0:T(8,128)} async-done(((f32[1024,512]{1,0:T(8,128)}), f32[1024,2048]{1,0:T(8,128)}) %all-gather.2.cloned.1.call-update) | async-done | bytes 8388624 | tf_op jit(solution)/shard_map/all_gather | solution.py:128
  578.8 31.8 %fusion.34 = f32[1024,1024]{1,0:T(8,128)} fusion(f32[1024,2048]{1,0:T(8,128)} %all-gather.2.cloned.1.call-done, f32[2048,1024]{1,0:T(8,128)} %bitcast.45), kind=kOutput, calls=%fused_computation.86 | convolution fusion | flops 25769803776 | bytes 20971520 | tf_op jit(solution)/shard_map/dot_general | solution.py:129
  (35 shorter events, 2.2 us)
Async XLA Ops:
  16.6 57.2 %all-to-all-start.1 = ((s32[8,192,1]{1,2,0:T(1,128)}), s32[8,192,1]{1,2,0:T(1,128)S(1)}, u32[]{:S(2)}, u32[]{:S(2)}) async-start(s32[8,192,1]{1,2,0:T(1,128)} %all_to_all.27), calls=%async_computation.1 | async-start | bytes 16384 | tf_op jit(solution)/shard_map/all_to_all | solution.py:108
  28.7 3.0 copy-start.5
  41.2 2.2 copy-start.1
  43.4 3.1 copy-start.3
  149.9 73.8 %all-to-all-start.2 = ((f32[1536,4,128]{2,1,0:T(4,128)}), f32[1536,4,128]{2,1,0:T(4,128)S(1)}, u32[]{:S(2)}, u32[]{:S(2)}) async-start(f32[1536,4,128]{2,1,0:T(4,128)} %get-tuple-element.41), calls=%async_computation.2 | async-start | bytes 6291456 | tf_op jit(solution)/shard_map/all_to_all | solution.py:120
  223.8 1.7 copy-start.2
  225.5 178.4 %all-to-all-start = ((f32[1536,4,128]{2,1,0:T(4,128)}), f32[1536,4,128]{2,1,0:T(4,128)}, u32[]{:S(2)}, u32[]{:S(2)}) async-start(f32[1536,4,128]{2,1,0:T(4,128)} %get-tuple-element.40), calls=%async_computation | async-start | bytes 6291456 | tf_op jit(solution)/shard_map/all_to_all | solution.py:122
  230.0 348.7 %all-gather.2.cloned.1.call-start = ((), (), s32[]{:S(2)}) async-start(), calls=%async_computation.5 | async-start | bytes 10485760 | tf_op jit(solution)/shard_map/all_gather | solution.py:128
  251.9 41.7 %collective-permute-start.2 = (f32[512,1024]{1,0:T(8,128)}, f32[512,1024]{1,0:T(8,128)}, u32[]{:S(2)}, u32[]{:S(2)}) collective-permute-start(f32[512,1024]{1,0:T(8,128)} %bitcast.42), channel_id=1, source_target_pairs={{0,3},{1,0},{2,1},{3,2},{4,7},{5,4},{6,5},{7,6},{8,11},{9,8},{10,9... | collective-permute-start | bytes 6291464 | tf_op jit(solution)/shard_map/ppermute | solution.py:74
  255.4 86.2 %collective-permute-start.1 = (f32[512,1024]{1,0:T(8,128)}, f32[512,1024]{1,0:T(8,128)}, u32[]{:S(2)}, u32[]{:S(2)}) collective-permute-start(f32[512,1024]{1,0:T(8,128)} %fusion.9), channel_id=1, source_target_pairs={{0,2},{1,3},{2,0},{3,1},{4,6},{5,7},{6,4},{7,5},{8,10},{9,11},{10,... | collective-permute-start | bytes 6291464 | tf_op jit(solution)/shard_map/ppermute | solution.py:74
  256.9 2.1 copy-start.4
  258.7 86.4 %collective-permute-start = (f32[512,1024]{1,0:T(8,128)}, f32[512,1024]{1,0:T(8,128)}, u32[]{:S(2)}, u32[]{:S(2)}) collective-permute-start(f32[512,1024]{1,0:T(8,128)} %fusion.10), channel_id=1, source_target_pairs={{0,1},{1,2},{2,3},{3,0},{4,5},{5,6},{6,7},{7,4},{8,9},{9,10},{10,1... | collective-permute-start | bytes 6291464 | tf_op jit(solution)/shard_map/ppermute | solution.py:74
  394.5 5.7 copy-start
Sparse Core Ops, SparseCore 0:
  521.4 57.3 all-gather.1
where the time goes:
time: 622 us; the launch traced here: 618 us
  waiting for transfers between devices  196 us (32%)
  blocking collectives  151 us (24%)
  local copies, waits for them, and re-layouts  114 us (18%)
  matrix products  70.7 us (11%)
  other arithmetic  55 us (9%)
  starting transfers between devices  17.4 us (3%)
  between operations  14.2 us (2%)
    ppermute x3, waiting for transfers between devices, per_device(): lax.ppermute(jnp.take(weight_blocks, dest, axis=1), 'head', [(src, (src +...  79 us
    all_to_all x1, blocking collectives, per_device(): lax.all_to_all(send_k, 'seq', split_axis=0, concat_axis=0, tiled=True)  76.2 us
    all_to_all x1, blocking collectives, per_device(): lax.all_to_all(result[picked], 'seq', split_axis=0, concat_axis=0, tiled=...  75.1 us
    all_to_all x1, waiting for transfers between devices, per_device(): lax.all_to_all(send_q, 'seq', split_axis=0, concat_axis=0, tiled=True)  59.2 us
    all_gather x1, waiting for transfers between devices, per_device(): gathered = lax.all_gather(mixed, 'head', axis=1, tiled=True)  57.5 us
    dot_general x1, matrix products, per_device(): jnp.dot(gathered, weight_cols, precision=lax.Precision.HIGHEST, preferred...  31.8 us
    gather x3, local copies, waits for them, and re-layouts, place(): return pieces[where_from]  20.7 us
    dot_general x1, matrix products, cluster_attention(): jnp.einsum('qhd,khd->hqk', query_c, key_c, precision=lax.Precision.HIGHEST)  20.7 us
  transfers between devices with their start and end apart: 7, of which 5 were waited for; matrix products, arithmetic and copies ran while one was open for 24% of the time, Pallas kernels for 0%

commit v1 on v0

--- a/solution.py
+++ b/solution.py
@@ -1,3 +1,4 @@
+import functools
 import math
 import jax
 import jax.numpy as jnp
@@ -12,6 +13,40 @@
 STRETCH = 4.0
 BETA_FAST = 32.0
 BETA_SLOW = 1.0
+
+
+def reach_rounds(s0, array_axis, packet):
+    seen_now = s0.shape
+    current_block = s0.reshape(
+        *seen_now[:array_axis], packet, seen_now[array_axis] // packet, *seen_now[array_axis + 1 :]
+    )
+    return jnp.moveaxis(current_block, array_axis, 0)
+
+
+def pack_lane(sample, on_dim):
+    sample = jnp.moveaxis(sample, 0, on_dim)
+    known = sample.shape
+    return sample.reshape(*known[:on_dim], known[on_dim] * known[on_dim + 1], *known[on_dim + 2 :])
+
+
+def press_rates(original, shard_axis, load, w_in):
+    vec_out, out_arr = (lax.axis_size(shard_axis), lax.axis_index(shard_axis))
+    v_next = reach_rounds(original, load, vec_out)
+    at = 1
+    fields = [v_next[out_arr]]
+    while at < vec_out:
+        block_out = v_next[out_arr ^ at]
+        fields.append(
+            lax.ppermute(
+                block_out, axis_name=shard_axis, perm=[(ii, ii ^ at) for ii in range(vec_out)]
+            )
+        )
+        at += 1
+    v_next = jnp.stack(fields, axis=0)[out_arr ^ jnp.arange(vec_out)]
+    return pack_lane(v_next, w_in)
+
+
+_see_rates = functools.partial(press_rates, shard_axis="seq", load=0, w_in=0)
 
 
 def yarn_tables(token_pos, width):
@@ -117,7 +152,7 @@
         return pieces[where_from]
 
     received = (
-        lax.all_to_all(send_q, "seq", split_axis=0, concat_axis=0, tiled=True),
+        _see_rates(send_q),
         lax.all_to_all(send_k, "seq", split_axis=0, concat_axis=0, tiled=True),
         lax.all_to_all(send_v, "seq", split_axis=0, concat_axis=0, tiled=True),
     )

time: 622 us -> 573 us (0.921)
  blocking collectives: 151 us -> 85.9 us
  starting transfers between devices: 17.4 us -> 35.9 us
  waiting for transfers between devices: 196 us -> 179 us
  local copies, waits for them, and re-layouts: 114 us -> 128 us
    ppermute x0 -> x7, waiting for transfers between devices: none -> 81.7 us  [press_rates(): lax.ppermute(block_out, axis_name=shard_axis, perm=[(ii, ii ^ at) for ii...]
    ppermute x3, waiting for transfers between devices: 79 us -> 0.01 us  [per_device(): lax.ppermute(jnp.take(weight_blocks, dest, axis=1), 'head', [(src, (src +...]
    all_to_all x1 -> x0, blocking collectives: 76.2 us -> none  [per_device(): lax.all_to_all(send_k, 'seq', split_axis=0, concat_axis=0, tiled=True)]
    all_to_all x1, waiting for transfers between devices: 59.2 us -> 39.2 us  [per_device(): lax.all_to_all(send_k, 'seq', split_axis=0, concat_axis=0, tiled=True)]
    ppermute x0 -> x7, starting transfers between devices: none -> 14.8 us  [press_rates(): lax.ppermute(block_out, axis_name=shard_axis, perm=[(ii, ii ^ at) for ii...]
    all_to_all x1, blocking collectives: 75.1 us -> 85.9 us  [per_device(): lax.all_to_all(result[picked], 'seq', split_axis=0, concat_axis=0, tiled=...]
    unnamed x15 -> x21, local copies, waits for them, and re-layouts: 12.9 us -> 18.8 us
  transfers between devices with their start and end apart: 7 -> 14, of which waited for: 5 -> 8; matrix products, arithmetic and copies ran while one was open for 24% -> 25% of each run, Pallas kernels for 0% -> 0%
where the time goes in v1:
time: 573 us; the launch traced here: 569 us
  waiting for transfers between devices  179 us (31%)
  local copies, waits for them, and re-layouts  128 us (22%)
  blocking collectives  85.9 us (15%)
  matrix products  67.3 us (12%)
  other arithmetic  58.8 us (10%)
  starting transfers between devices  35.9 us (6%)
  between operations  13.9 us (2%)
    all_to_all x1, blocking collectives, per_device(): lax.all_to_all(result[picked], 'seq', split_axis=0, concat_axis=0, tiled=...  85.9 us
    ppermute x7, waiting for transfers between devices, press_rates(): lax.ppermute(block_out, axis_name=shard_axis, perm=[(ii, ii ^ at) for ii...  81.7 us
    all_gather x1, waiting for transfers between devices, per_device(): gathered = lax.all_gather(mixed, 'head', axis=1, tiled=True)  57.5 us
    all_to_all x1, waiting for transfers between devices, per_device(): lax.all_to_all(send_k, 'seq', split_axis=0, concat_axis=0, tiled=True)  39.2 us
    dot_general x1, matrix products, per_device(): jnp.dot(gathered, weight_cols, precision=lax.Precision.HIGHEST, preferred...  31.8 us
    gather x3, local copies, waits for them, and re-layouts, place(): return pieces[where_from]  21.1 us
    dynamic_slice x1, other arithmetic, per_device(): piece = weight_blocks[:, head_index]  20 us
    unnamed x21, local copies, waits for them, and re-layouts  18.8 us
  transfers between devices with their start and end apart: 14, of which 8 were waited for; matrix products, arithmetic and copies ran while one was open for 25% of the time, Pallas kernels for 0%

profile of v1, /device:TPU:0, one launch (start us, length us, event | category | flops | bytes accessed | tf_op | source)
XLA Modules:
  0.0 568.6 jit_solution(16265885518938642102)
XLA Ops:
  7.2 2.3 reduce-window.6
  11.4 4.5 scatter_custom_fusion.1
  16.6 7.3 %all-to-all-start.1 = ((s32[8,192,1]{1,2,0:T(1,128)}), s32[8,192,1]{1,2,0:T(1,128)S(1)}, u32[]{:S(2)}, u32[]{:S(2)}) async-start(s32[8,192,1]{1,2,0:T(1,128)} %all_to_all.23), calls=%async_computation.1 | async-start | bytes 16384 | tf_op jit(solution)/shard_map/all_to_all | solution.py:143
  23.9 1.9 reshape.249
  25.8 2.9 reshape.250
  28.7 2.9 reshape.251
  31.6 4.5 scatter_custom_fusion
  36.1 4.6 slice_negate_fusion
  40.8 1.9 multiply_cosine_fusion
  43.0 3.0 fusion.7
  46.1 5.3 select_maximum_fusion
  52.2 12.0 %gather_fusion = f32[1536,12,128]{2,1,0:T(8,128)} fusion(f32[1025,12,128]{2,1,0:T(8,128)} %select_maximum_fusion, s32[2048]{0:T(1024)S(1)} %get-tuple-element.70), kind=kCustom, calls=%fused_computation | custom fusion | bytes 18880512 | tf_op jit(solution)/shard_map/gather | solution.py:138
  64.1 10.0 %fusion.34 = (f32[1536,4,128]{2,1,0:T(4,128)}, f32[1536,4,128]{2,1,0:T(4,128)S(1)}, f32[1536,4,128]{2,1,0:T(4,128)}) fusion(f32[1536,12,128]{2,1,0:T(8,128)} %gather_fusion), kind=kLoop, calls=%fused_computation.104 | loop fusion | bytes 18874368 | tf_op jit(solution)/shard_map/slice | solution.py:141
  74.1 6.3 %all-to-all-start.2 = ((f32[1536,4,128]{2,1,0:T(4,128)}), f32[1536,4,128]{2,1,0:T(4,128)}, u32[]{:S(2)}, u32[]{:S(2)}) async-start(f32[1536,4,128]{2,1,0:T(4,128)} %get-tuple-element.42), calls=%async_computation.2 | async-start | bytes 6291456 | tf_op jit(solution)/shard_map/all_to_all | solution.py:156
  80.4 10.8 %reshape.255 = f32[512,4,1024]{2,1,0:T(4,128)} reshape(f32[512,4096]{1,0:T(8,128)} %param.15) | data formatting | bytes 16777216 | tf_op jit(solution)/shard_map/reshape | solution.py:102
  91.3 20.0 %constant_dynamic-slice_fusion.2 = (f32[512,1,1024]{2,1,0:T(1,128)}, f32[512,1,1024]{2,1,0:T(1,128)}, f32[512,1,1024]{2,1,0:T(1,128)}, f32[512,1,1024]{2,1,0:T(1,128)}) fusion(f32[512,4,1024]{2,1,0:T(4,128)} %reshape.255, s32[]{:T(128)S(6)} %select_n.141, s32[]{:T(128)S(6)} %select_n.158, s32[]{:T(128)S(6)} %select_n.162, pred[]{:T(512)S(6)} %and.54, ...), kind=kLoop, calls=%fused_computation.89 | loop fusion | flops 524288 | bytes 16777232 | tf_op jit(solution)/shard_map/dynamic_slice | solution.py:106
  111.3 39.2 %all-to-all-done.2 = f32[1536,4,128]{2,1,0:T(4,128)} async-done(((f32[1536,4,128]{2,1,0:T(4,128)}), f32[1536,4,128]{2,1,0:T(4,128)}, u32[]{:S(2)}, u32[]{:S(2)}) %all-to-all-start.2) | async-done | bytes 3145760 | tf_op jit(solution)/shard_map/all_to_all | solution.py:156
  150.6 4.5 all-to-all-start
  155.1 3.5 fusion.10
  158.6 3.6 fusion.9
  167.0 3.4 copy.57
  173.2 1.8 collective-permute-start
  176.9 6.3 %scatter_custom_fusion.2 = s32[1024]{0:T(1024)S(1)} fusion(s32[1536]{0:T(1024)} %get-tuple-element.37, s32[1536]{0:T(1024)S(1)} %iota.46, s32[]{:T(128)} %constant.138.clone.1), kind=kCustom, calls=%fused_computation.95 | custom fusion | bytes 4608 | tf_op jit(solution)/shard_map/scatter | solution.py:148
  183.2 7.8 %collective-permute-done = f32[192,4,128]{2,1,0:T(4,128)S(1)} collective-permute-done((f32[192,4,128]{2,1,0:T(4,128)}, f32[192,4,128]{2,1,0:T(4,128)S(1)}, u32[]{:S(2)}, u32[]{:S(2)}) %collective-permute-start) | collective-permute-done | bytes 393248 | tf_op jit(solution)/shard_map/ppermute | solution.py:40
  192.7 23.6 %collective-permute-done.1 = f32[192,4,128]{2,1,0:T(4,128)S(1)} collective-permute-done((f32[192,4,128]{2,1,0:T(4,128)}, f32[192,4,128]{2,1,0:T(4,128)S(1)}, u32[]{:S(2)}, u32[]{:S(2)}) %collective-permute-start.1) | collective-permute-done | bytes 393248 | tf_op jit(solution)/shard_map/ppermute | solution.py:40
  216.3 4.0 collective-permute-start.3
  221.0 3.7 collective-permute-done.2
  224.7 4.9 collective-permute-start.4
  230.4 22.0 %collective-permute-done.3 = f32[192,4,128]{2,1,0:T(4,128)S(1)} collective-permute-done((f32[192,4,128]{2,1,0:T(4,128)}, f32[192,4,128]{2,1,0:T(4,128)S(1)}, u32[]{:S(2)}, u32[]{:S(2)}) %collective-permute-start.3) | collective-permute-done | bytes 393248 | tf_op jit(solution)/shard_map/ppermute | solution.py:40
  253.6 15.7 %collective-permute-done.4 = f32[192,4,128]{2,1,0:T(4,128)S(1)} collective-permute-done((f32[192,4,128]{2,1,0:T(4,128)}, f32[192,4,128]{2,1,0:T(4,128)S(1)}, u32[]{:S(2)}, u32[]{:S(2)}) %collective-permute-start.4) | collective-permute-done | bytes 393248 | tf_op jit(solution)/shard_map/ppermute | solution.py:40
  272.1 8.9 %collective-permute-done.6 = f32[192,4,128]{2,1,0:T(4,128)S(1)} collective-permute-done((f32[192,4,128]{2,1,0:T(4,128)S(1)}, f32[192,4,128]{2,1,0:T(4,128)S(1)}, u32[]{:S(2)}, u32[]{:S(2)}) %collective-permute-start.6) | collective-permute-done | bytes 393248 | tf_op jit(solution)/shard_map/ppermute | solution.py:40
  281.9 5.9 %gather_fusion.2 = f32[8,192,4,128]{3,2,1,0:T(4,128)} fusion(f32[8,192,4,128]{3,2,1,0:T(4,128)} %bitcast_dynamic-update-slice_fusion, s32[1024]{0:T(1024)} %pad_clamp_fusion.3), kind=kCustom, calls=%fused_computation.2 | custom fusion | bytes 6291488 | tf_op jit(solution)/shard_map/gather | solution.py:45
  287.8 5.4 gather_fusion.3
  293.3 6.0 %pad_maximum_fusion = f32[4,512,1024]{2,1,0:T(8,128)} fusion(f32[1,512,1024]{2,1,0:T(8,128)} %bitcast.27, f32[1,512,1024]{2,1,0:T(8,128)} %bitcast.26, f32[1,512,1024]{2,1,0:T(8,128)} %bitcast.24, f32[1,512,1024]{2,1,0:T(8,128)} %bitcast.82), kind=kLoop, calls=%fused_computation.19 | loop fusion | flops 6291456 | bytes 16777216 | tf_op jit(solution)/shard_map/stack | solution.py:115
  299.3 7.8 %gather_fusion.5 = f32[4,512,1024]{2,1,0:T(8,128)} fusion(f32[4,512,1024]{2,1,0:T(8,128)} %pad_maximum_fusion, s32[1024]{0:T(1024)} %pad_clamp_fusion.2), kind=kCustom, calls=%fused_computation.5 | custom fusion | bytes 16777232 | tf_op jit(solution)/shard_map/gather | solution.py:117
  307.1 10.2 %gather_fusion.4 = f32[1024,4,128]{2,1,0:T(4,128)} fusion(f32[1536,4,128]{2,1,0:T(4,128)} %all-to-all-done.2, s32[1024]{0:T(1024)S(1)} %fusion.22), kind=kCustom, calls=%fused_computation.4 | custom fusion | bytes 4198400 | tf_op jit(solution)/shard_map/gather | solution.py:152
  317.3 17.5 %fusion = (f32[4,1024]{1,0:T(4,128)S(1)}, f32[4,1024,1024]{1,2,0:T(8,128)S(1)}) fusion(pred[1024,1024]{0,1:T(8,128)(4,1)S(1)} %iota_compare_fusion.1, f32[1024,4,128]{2,1,0:T(4,128)} %gather_fusion.4, f32[1024,4,128]{2,1,0:T(4,128)S(1)} %gather_fusion.3), kind=kOutput, calls=%fused_computation.13 | convolution fusion | flops 6455029760 | bytes 22036480 | tf_op jit(solution)/shard_map/while/body/eval_jaxpr/qhd,khd->hqk/dot_general | solution.py:75
  334.8 5.7 %copy-done = f32[4,1024,1024]{1,2,0:T(8,128)} copy-done((f32[4,1024,1024]{1,2,0:T(8,128)}, f32[4,1024,1024]{1,2,0:T(8,128)S(1)}, u32[]{:S(2)}) %copy-start) | copy-done | bytes 16777240
  340.5 3.6 fusion.1
  344.2 5.4 gather_fusion.1
  349.6 17.9 %bitcast_divide_fusion = f32[1024,4,128]{0,2,1:T(8,128)} fusion(f32[1024,4]{0,1:T(4,128)S(1)} %bitcast.85, f32[4,1024,1024]{1,2,0:T(8,128)} %copy-done, f32[4,1024]{1,0:T(4,128)S(1)} %get-tuple-element.63, pred[1024,1024]{0,1:T(8,128)(4,1)S(1)} %iota_compare_fusion.1, f32[1024,4,128]{2,1,0:T(4,128)S(1)} %gather_fusion.1), kind=kOutput, calls=%fused_computation.39 | convolution fusion | flops 6455558144 | bytes 22052864 | tf_op jit(solution)/shard_map/while/body/eval_jaxpr/hqk,khd->qhd/dot_general | solution.py:83
  367.5 2.0 copy.25
  369.6 5.7 %gather_fusion.6 = f32[1536,4,128]{2,1,0:T(4,128)} fusion(f32[1024,4,128]{2,1,0:T(4,128)S(1)} %copy.25, s32[2048]{0:T(1024)S(1)} %get-tuple-element.69), kind=kCustom, calls=%fused_computation.6 | custom fusion | bytes 6297600 | tf_op jit(solution)/shard_map/gather | solution.py:161
  375.3 85.9 %all_to_all.28 = f32[1536,4,128]{2,1,0:T(4,128)S(1)} all-to-all(f32[1536,4,128]{2,1,0:T(4,128)} %gather_fusion.6), channel_id=1, replica_groups=mesh['seq'=8,'head'=4] {'seq'}, dimensions={0} | all-to-all | bytes 6291456 | tf_op jit(solution)/shard_map/all_to_all | solution.py:161
  461.1 7.9 %gather_fusion.7 = f32[1024,4,128]{2,1,0:T(4,128)} fusion(f32[1536,4,128]{2,1,0:T(4,128)S(1)} %all_to_all.28, s32[1024]{0:T(1024)S(1)} %get-tuple-element.38), kind=kCustom, calls=%fused_computation.7 | custom fusion | bytes 4198400 | tf_op jit(solution)/shard_map/gather | solution.py:162
  469.1 3.1 copy.55
  472.2 57.5 %all-gather.2.cloned.1.call-done = f32[1024,2048]{1,0:T(8,128)} async-done(((f32[1024,512]{1,0:T(8,128)}), f32[1024,2048]{1,0:T(8,128)}) %all-gather.2.cloned.1.call-update) | async-done | bytes 8388624 | tf_op jit(solution)/shard_map/all_gather | solution.py:163
  529.7 31.8 %fusion.35 = f32[1024,1024]{1,0:T(8,128)} fusion(f32[1024,2048]{1,0:T(8,128)} %all-gather.2.cloned.1.call-done, f32[2048,1024]{1,0:T(8,128)} %bitcast.79), kind=kOutput, calls=%fused_computation.105 | convolution fusion | flops 25769803776 | bytes 20971520 | tf_op jit(solution)/shard_map/dot_general | solution.py:164
  (58 shorter events, 21.9 us)
Async XLA Ops:
  16.6 34.8 %all-to-all-start.1 = ((s32[8,192,1]{1,2,0:T(1,128)}), s32[8,192,1]{1,2,0:T(1,128)S(1)}, u32[]{:S(2)}, u32[]{:S(2)}) async-start(s32[8,192,1]{1,2,0:T(1,128)} %all_to_all.23), calls=%async_computation.1 | async-start | bytes 16384 | tf_op jit(solution)/shard_map/all_to_all | solution.py:143
  23.8 4.9 copy-start.5
  40.8 2.2 copy-start.1
  43.0 3.1 copy-start.2
  74.1 76.5 %all-to-all-start.2 = ((f32[1536,4,128]{2,1,0:T(4,128)}), f32[1536,4,128]{2,1,0:T(4,128)}, u32[]{:S(2)}, u32[]{:S(2)}) async-start(f32[1536,4,128]{2,1,0:T(4,128)} %get-tuple-element.42), calls=%async_computation.2 | async-start | bytes 6291456 | tf_op jit(solution)/shard_map/all_to_all | solution.py:156
  150.6 193.6 %all-to-all-start = ((f32[1536,4,128]{2,1,0:T(4,128)}), f32[1536,4,128]{2,1,0:T(4,128)}, u32[]{:S(2)}, u32[]{:S(2)}) async-start(f32[1536,4,128]{2,1,0:T(4,128)} %get-tuple-element.40), calls=%async_computation | async-start | bytes 6291456 | tf_op jit(solution)/shard_map/all_to_all | solution.py:157
  155.1 374.6 %all-gather.2.cloned.1.call-start = ((), (), s32[]{:S(2)}) async-start(), calls=%async_computation.4 | async-start | bytes 10485760 | tf_op jit(solution)/shard_map/all_gather | solution.py:163
  158.6 134.6 %collective-permute-start.7 = (f32[512,1024]{1,0:T(8,128)}, f32[512,1024]{1,0:T(8,128)}, u32[]{:S(2)}, u32[]{:S(2)}) collective-permute-start(f32[512,1024]{1,0:T(8,128)} %fusion.10), channel_id=1, source_target_pairs={{0,1},{1,2},{2,3},{3,0},{4,5},{5,6},{6,7},{7,4},{8,9},{9,10},{10,1... | collective-permute-start | bytes 6291464 | tf_op jit(solution)/shard_map/ppermute | solution.py:109
  158.6 5.1 copy-start.3
  162.2 131.0 %collective-permute-start.8 = (f32[512,1024]{1,0:T(8,128)}, f32[512,1024]{1,0:T(8,128)}, u32[]{:S(2)}, u32[]{:S(2)}) collective-permute-start(f32[512,1024]{1,0:T(8,128)} %fusion.9), channel_id=1, source_target_pairs={{0,2},{1,3},{2,0},{3,1},{4,6},{5,7},{6,4},{7,5},{8,10},{9,11},{10,... | collective-permute-start | bytes 6291464 | tf_op jit(solution)/shard_map/ppermute | solution.py:109
  165.6 127.7 %collective-permute-start.9 = (f32[512,1024]{1,0:T(8,128)}, f32[512,1024]{1,0:T(8,128)}, u32[]{:S(2)}, u32[]{:S(2)}) collective-permute-start(f32[512,1024]{1,0:T(8,128)} %bitcast.74), channel_id=1, source_target_pairs={{0,3},{1,0},{2,1},{3,2},{4,7},{5,4},{6,5},{7,6},{8,11},{9,8},{10,9... | collective-permute-start | bytes 6291464 | tf_op jit(solution)/shard_map/ppermute | solution.py:109
  173.2 79.2 %copy-start.4 = (f32[192,4,128]{2,1,0:T(4,128)S(1)}, f32[192,4,128]{2,1,0:T(4,128)}, u32[]{:S(2)}) copy-start(f32[192,4,128]{2,1,0:T(4,128)} %get-tuple-element.48) | copy-start | bytes 1179652
  173.2 17.9 %collective-permute-start = (f32[192,4,128]{2,1,0:T(4,128)}, f32[192,4,128]{2,1,0:T(4,128)S(1)}, u32[]{:S(2)}, u32[]{:S(2)}) collective-permute-start(f32[192,4,128]{2,1,0:T(4,128)} %get-tuple-element.53), channel_id=1, source_target_pairs={{0,4},{4,0},{8,12},{12,8},{16,20},{20,16},{24,28},{28,24},{1,5},{5... | collective-permute-start | bytes 1179656 | tf_op jit(solution)/shard_map/ppermute | solution.py:40
  175.3 40.9 %collective-permute-start.1 = (f32[192,4,128]{2,1,0:T(4,128)}, f32[192,4,128]{2,1,0:T(4,128)S(1)}, u32[]{:S(2)}, u32[]{:S(2)}) collective-permute-start(f32[192,4,128]{2,1,0:T(4,128)} %get-tuple-element.52), channel_id=1, source_target_pairs={{0,8},{4,12},{8,0},{12,4},{16,24},{20,28},{24,16},{28,20},{1,9},{5... | collective-permute-start | bytes 1179656 | tf_op jit(solution)/shard_map/ppermute | solution.py:40
  191.0 33.6 %collective-permute-start.2 = (f32[192,4,128]{2,1,0:T(4,128)}, f32[192,4,128]{2,1,0:T(4,128)S(1)}, u32[]{:S(2)}, u32[]{:S(2)}) collective-permute-start(f32[192,4,128]{2,1,0:T(4,128)} %get-tuple-element.51), channel_id=1, source_target_pairs={{0,12},{4,8},{8,4},{12,0},{16,28},{20,24},{24,20},{28,16},{1,13},{... | collective-permute-start | bytes 1179656 | tf_op jit(solution)/shard_map/ppermute | solution.py:40
  216.3 36.1 %collective-permute-start.3 = (f32[192,4,128]{2,1,0:T(4,128)}, f32[192,4,128]{2,1,0:T(4,128)S(1)}, u32[]{:S(2)}, u32[]{:S(2)}) collective-permute-start(f32[192,4,128]{2,1,0:T(4,128)} %get-tuple-element.50), channel_id=1, source_target_pairs={{0,16},{4,20},{8,24},{12,28},{16,0},{20,4},{24,8},{28,12},{1,17},{... | collective-permute-start | bytes 1179656 | tf_op jit(solution)/shard_map/ppermute | solution.py:40
  224.7 44.6 %collective-permute-start.4 = (f32[192,4,128]{2,1,0:T(4,128)}, f32[192,4,128]{2,1,0:T(4,128)S(1)}, u32[]{:S(2)}, u32[]{:S(2)}) collective-permute-start(f32[192,4,128]{2,1,0:T(4,128)} %get-tuple-element.49), channel_id=1, source_target_pairs={{0,20},{4,16},{8,28},{12,24},{16,4},{20,0},{24,12},{28,8},{1,21},{... | collective-permute-start | bytes 1179656 | tf_op jit(solution)/shard_map/ppermute | solution.py:40
  252.4 19.0 %collective-permute-start.5 = (f32[192,4,128]{2,1,0:T(4,128)S(1)}, f32[192,4,128]{2,1,0:T(4,128)S(1)}, u32[]{:S(2)}, u32[]{:S(2)}) collective-permute-start(f32[192,4,128]{2,1,0:T(4,128)S(1)} %copy-done.4), channel_id=1, source_target_pairs={{0,24},{4,28},{8,16},{12,20},{16,8},{20,12},{24,0},{28,4},{1,25},{... | collective-permute-start | bytes 1179656 | tf_op jit(solution)/shard_map/ppermute | solution.py:40
  269.3 11.8 %collective-permute-start.6 = (f32[192,4,128]{2,1,0:T(4,128)S(1)}, f32[192,4,128]{2,1,0:T(4,128)S(1)}, u32[]{:S(2)}, u32[]{:S(2)}) collective-permute-start(f32[192,4,128]{2,1,0:T(4,128)S(1)} %get-tuple-element.47), channel_id=1, source_target_pairs={{0,28},{4,24},{8,20},{12,16},{16,12},{20,8},{24,4},{28,0},{1,29},{... | collective-permute-start | bytes 1179656 | tf_op jit(solution)/shard_map/ppermute | solution.py:40
  334.8 5.7 %copy-start = (f32[4,1024,1024]{1,2,0:T(8,128)}, f32[4,1024,1024]{1,2,0:T(8,128)S(1)}, u32[]{:S(2)}) copy-start(f32[4,1024,1024]{1,2,0:T(8,128)S(1)} %get-tuple-element.64) | copy-start | bytes 50331652
Sparse Core Ops, SparseCore 0:
  472.3 57.3 all-gather.1
